TPU v7x, 512 devices: a whole 4x4x16 slice. The times are simulated.
512 devices in a mesh: row: 16 (over y, x_lo, core), col: 32 (over z, x_hi).
Axes of the slice: x: 4 (x_hi: 2, x_lo: 2; x = x_hi * 2 + x_lo), y: 4, z: 16, core: 2. Of those that a mesh axis runs over, the one named last changes fastest.
Arguments:
- velocity: bfloat16 [3, 512, 512, 512], P(None, 'row', 'col'), may hold values from -6 to 6
- wall_slope: bfloat16 [512, 512], replicated, may hold values from -0.25 to 0.25
- wall_diffusion: bfloat16 [512, 512], replicated, may hold values from -0.25 to 0.25
- span_slope: bfloat16 [512, 512], replicated, may hold values from -0.25 to 0.25
- span_diffusion: bfloat16 [512, 512], replicated, may hold values from -0.25 to 0.25
Outputs:
- tendency: bfloat16 [3, 512, 512, 512], P(None, 'row', 'col')
All inputs are finite; a program needn't handle non-finite values.
Results may differ from a plain program's by a relative error of at most 0.0051.
Values may be sent and summed in bfloat16 or wider, within the bound.
No kernel may reach another device: no remote copies, remote signals or barrier semaphores. Data moves between devices by JAX's collectives and lax.ppermute only.
A program may use at most 128 MiB of HBM per device.

v0:
```python
import jax
import jax.numpy as jnp
from jax import lax
from jax.sharding import Mesh, PartitionSpec as P


ROW_PARTS = (("y", 4), ("xl", 2), ("core", 2))
COL_PARTS = (("z", 16), ("xh", 2))
COLS = ("z", "xh")


def rate_of_change(slope, diffusion, lines, carrier):
    gradient = jnp.einsum("ij,cjm->cim", slope, lines, preferred_element_type=jnp.float32)
    curvature = jnp.einsum("ij,cjm->cim", diffusion, lines, preferred_element_type=jnp.float32)
    term = curvature - carrier[None].astype(jnp.float32) * gradient
    return term.astype(jnp.bfloat16)


def exchange(blocks, axes):
    return lax.all_to_all(blocks, axes, split_axis=0, concat_axis=0, tiled=True)


def take_at(x, i, axis):
    return lax.dynamic_index_in_dim(x, i, axis, keepdims=False)


def swap(x, axis):
    return lax.ppermute(x, axis, [(0, 1), (1, 0)])


def in_order(mine, other, me):
    first = jnp.where(me == 0, mine, other)
    second = jnp.where(me == 0, other, mine)
    return jnp.stack([first, second], axis=0)


def rotate_in(pieces, me, n):
    order = (me - jnp.arange(n)) % n
    return jnp.take(pieces, order, axis=0)


def both_terms(velocity, wall_slope, wall_diffusion, span_slope, span_diffusion):
    ny, nxl, ncore = (lax.axis_size(n) for n, _ in ROW_PARTS)
    my_y, my_xl, my_core = (lax.axis_index(n) for n, _ in ROW_PARTS)
    column_count = lax.axis_size(COLS)
    comps, wall_local, span_local, stream_len = velocity.shape
    row_count = ny * nxl * ncore
    wall_total = wall_local * row_count
    span_total = span_local * column_count
    ws = wall_local // column_count
    zr = span_local // row_count

    v = velocity.reshape(comps, wall_local, ny, nxl, ncore, zr, stream_len)
    keep = take_at(v, my_core, 4)
    got = swap(take_at(v, 1 - my_core, 4), "core")
    s1 = in_order(keep, got, my_core)
    keep = take_at(s1, my_xl, 4)
    got = swap(take_at(s1, 1 - my_xl, 4), "xl")
    s2 = in_order(keep, got, my_xl)
    pieces = [take_at(s2, my_y, 4)]
    for s in range(1, ny):
        part = take_at(s2, (my_y + s) % ny, 4)
        pieces.append(lax.ppermute(part, "y", [(i, (i + s) % ny) for i in range(ny)]))
    s3 = rotate_in(jnp.stack(pieces, axis=0), my_y, ny)
    wall_lines = s3.transpose(3, 5, 0, 1, 2, 4, 6).reshape(comps, zr, wall_total, stream_len)

    wall_parts = []
    for k in range(zr):
        lines = wall_lines[:, k]
        wall_parts.append(rate_of_change(wall_slope, wall_diffusion, lines, lines[1]))
    wall_term = jnp.stack(wall_parts, axis=1)

    w = wall_term.reshape(comps, zr, ny, nxl, ncore, wall_local, stream_len)
    pieces = [take_at(w, my_y, 2)]
    for s in range(1, ny):
        part = take_at(w, (my_y + s) % ny, 2)
        pieces.append(lax.ppermute(part, "y", [(i, (i + s) % ny) for i in range(ny)]))
    b3 = rotate_in(jnp.stack(pieces, axis=0), my_y, ny)
    keep = take_at(b3, my_xl, 3)
    got = swap(take_at(b3, 1 - my_xl, 3), "xl")
    b2 = in_order(keep, got, my_xl)
    keep = take_at(b2, my_core, 4)
    got = swap(take_at(b2, 1 - my_core, 4), "core")
    b1 = in_order(keep, got, my_core)
    wall_back = b1.transpose(3, 5, 2, 1, 0, 4, 6).reshape(comps, wall_local, span_local, stream_len)

    send = velocity.reshape(comps, column_count, ws, span_local, stream_len).transpose(1, 0, 2, 3, 4)
    got = exchange(send, COLS)
    span_lines = got.transpose(1, 2, 0, 3, 4).reshape(comps, ws, span_total, stream_len)
    span_parts = []
    for k in range(ws):
        lines = span_lines[:, k]
        span_parts.append(rate_of_change(span_slope, span_diffusion, lines, lines[2]))
    span_term = jnp.stack(span_parts, axis=1)
    send = span_term.reshape(comps, ws, column_count, span_local, stream_len).transpose(2, 0, 1, 3, 4)
    span_back = exchange(send, COLS)
    span_back = span_back.transpose(1, 0, 2, 3, 4).reshape(comps, wall_local, span_local, stream_len)

    summed = wall_back.astype(jnp.float32) + span_back.astype(jnp.float32)
    return summed.astype(jnp.bfloat16)


def solution(mesh):
    names = tuple(n for n, _ in ROW_PARTS + COL_PARTS)
    sizes = tuple(s for _, s in ROW_PARTS + COL_PARTS)
    fine = Mesh(mesh.devices.reshape(sizes), names)
    rows = tuple(n for n, _ in ROW_PARTS)
    in_specs = (P(None, rows, COLS, None), P(), P(), P(), P())
    out_specs = P(None, rows, COLS, None)
    return jax.shard_map(both_terms, mesh=fine, in_specs=in_specs, out_specs=out_specs, check_vma=False)
```

profile of v0, /device:TPU:1, one launch (start us, length us, event | category | flops | bytes accessed | tf_op | source)
XLA Modules:
  0.0 207.6 jit_solution(13994475300147187828)
XLA Ops:
  0.0 2.7 %copy.53 = bf16[3,32,16,512]{3,2,0,1:T(8,128)(2,1)} copy(bf16[3,32,16,512]{3,2,1,0:T(8,128)(2,1)} %param.5) | data formatting | bytes 3145728 | tf_op args[0]
  2.7 18.6 %all-to-all-start = ((bf16[32,3,1,16,512]{4,3,1,2,0:T(8,128)(2,1)}), bf16[32,3,1,16,512]{4,3,1,2,0:T(8,128)(2,1)}, u32[]{:S(2)}, u32[]{:S(2)}) async-start(bf16[32,3,1,16,512]{4,3,1,2,0:T(8,128)(2,1)} %bitcast.165), calls=%async_computation | async-start | bytes 3145728 | tf_op jit(solution)/shard_map/all_to_all | solution.py:20
  21.3 2.3 %copy.32 = bf16[3,32,16,512]{3,1,2,0:T(8,128)(2,1)S(1)} copy(bf16[3,32,16,512]{3,2,1,0:T(8,128)(2,1)} %param.5) | data formatting | bytes 3145728 | tf_op args[0]
  23.7 2.9 %collective-permute-start = (bf16[3,32,4,2,1,512]{5,1,3,2,0,4:T(8,128)(2,1)S(1)}, bf16[3,32,4,2,1,512]{5,1,3,2,0,4:T(8,128)(2,1)}, u32[]{:S(2)}, u32[]{:S(2)}) collective-permute-start(bf16[3,32,4,2,1,512]{5,1,3,2,0,4:T(8,128)(2,1)S(1)} %dynamic-slice_bitcast_fusion.1), channel_id=1, source_target_pairs={{0,32},{32,0},{1,33},{33,1},{2,34},{34,2},{3,35},{35,3},{4,36},{36... | collective-permute-start | bytes 2359304 | tf_op jit(solution)/shard_map/ppermute | solution.py:28
  26.6 2.0 collective-permute-done
  32.3 2.2 %collective-permute-start.1 = (bf16[2,3,32,4,1,512]{5,2,3,1,0,4:T(8,128)(2,1)}, bf16[2,3,32,4,1,512]{5,2,3,1,0,4:T(8,128)(2,1)S(1)}, u32[]{:S(2)}, u32[]{:S(2)}) collective-permute-start(bf16[2,3,32,4,1,512]{5,2,3,1,0,4:T(8,128)(2,1)} %fusion.13), channel_id=1, source_target_pairs={{0,64},{64,0},{1,65},{65,1},{2,66},{66,2},{3,67},{67,3},{4,68},{68... | collective-permute-start | bytes 2359304 | tf_op jit(solution)/shard_map/ppermute | solution.py:28
  34.5 61.6 %all-to-all-done = bf16[32,3,1,16,512]{4,3,1,2,0:T(8,128)(2,1)} async-done(((bf16[32,3,1,16,512]{4,3,1,2,0:T(8,128)(2,1)}), bf16[32,3,1,16,512]{4,3,1,2,0:T(8,128)(2,1)}, u32[]{:S(2)}, u32[]{:S(2)}) %all-to-all-start) | async-done | bytes 1572896 | tf_op jit(solution)/shard_map/all_to_all | solution.py:20
  97.3 1.5 copy.45
  102.2 7.9 %all-to-all-start.1 = ((bf16[32,3,1,16,512]{4,3,1,2,0:T(8,128)(2,1)}), bf16[32,3,1,16,512]{4,3,1,2,0:T(8,128)(2,1)}, u32[]{:S(2)}, u32[]{:S(2)}) async-start(bf16[32,3,1,16,512]{4,3,1,2,0:T(8,128)(2,1)} %bitcast.174), calls=%async_computation.1 | async-start | bytes 3145728 | tf_op jit(solution)/shard_map/all_to_all | solution.py:20
  110.5 3.2 %collective-permute-start.2 = (bf16[2,2,3,32,1,512]{5,3,2,1,0,4:T(8,128)(2,1)S(1)}, bf16[2,2,3,32,1,512]{5,3,2,1,0,4:T(8,128)(2,1)S(1)}, u32[]{:S(2)}, u32[]{:S(2)}) collective-permute-start(bf16[2,2,3,32,1,512]{5,3,2,1,0,4:T(8,128)(2,1)S(1)} %get-tuple-element.14), channel_id=1, source_target_pairs={{0,128},{128,256},{256,384},{384,0},{1,129},{129,257},{257,385},{3... | collective-permute-start | bytes 1179656 | tf_op jit(solution)/shard_map/ppermute | solution.py:63
  113.7 4.5 %collective-permute-start.3 = (bf16[2,2,3,32,1,512]{5,3,2,1,0,4:T(8,128)(2,1)S(1)}, bf16[2,2,3,32,1,512]{5,3,2,1,0,4:T(8,128)(2,1)S(1)}, u32[]{:S(2)}, u32[]{:S(2)}) collective-permute-start(bf16[2,2,3,32,1,512]{5,3,2,1,0,4:T(8,128)(2,1)S(1)} %get-tuple-element.15), channel_id=1, source_target_pairs={{0,256},{128,384},{256,0},{384,128},{1,257},{129,385},{257,1},{385... | collective-permute-start | bytes 1179656 | tf_op jit(solution)/shard_map/ppermute | solution.py:63
  118.3 3.0 %collective-permute-start.4 = (bf16[2,2,3,32,1,512]{5,3,2,1,0,4:T(8,128)(2,1)S(1)}, bf16[2,2,3,32,1,512]{5,3,2,1,0,4:T(8,128)(2,1)S(1)}, u32[]{:S(2)}, u32[]{:S(2)}) collective-permute-start(bf16[2,2,3,32,1,512]{5,3,2,1,0,4:T(8,128)(2,1)S(1)} %get-tuple-element.16), channel_id=1, source_target_pairs={{0,384},{128,0},{256,128},{384,256},{1,385},{129,1},{257,129},{385... | collective-permute-start | bytes 1179656 | tf_op jit(solution)/shard_map/ppermute | solution.py:63
  121.3 2.0 collective-permute-done.2
  123.3 9.5 %collective-permute-done.3 = bf16[2,2,3,32,1,512]{5,3,2,1,0,4:T(8,128)(2,1)S(1)} collective-permute-done((bf16[2,2,3,32,1,512]{5,3,2,1,0,4:T(8,128)(2,1)S(1)}, bf16[2,2,3,32,1,512]{5,3,2,1,0,4:T(8,128)(2,1)S(1)}, u32[]{:S(2)}, u32[]{:S(2)}) %collective-permute-start.3) | collective-permute-done | bytes 393248 | tf_op jit(solution)/shard_map/ppermute | solution.py:63
  132.8 1.8 collective-permute-done.4
  134.8 1.8 gather_fusion
  136.6 1.6 fusion.5
  141.6 5.4 %collective-permute-start.7 = (bf16[3,1,2,2,32,512]{5,4,3,2,0,1:T(8,128)(2,1)S(1)}, bf16[3,1,2,2,32,512]{5,4,3,2,0,1:T(8,128)(2,1)S(1)}, u32[]{:S(2)}, u32[]{:S(2)}) collective-permute-start(bf16[3,1,2,2,32,512]{5,4,3,2,0,1:T(8,128)(2,1)S(1)} %get-tuple-element.10), channel_id=1, source_target_pairs={{0,384},{128,0},{256,128},{384,256},{1,385},{129,1},{257,129},{385... | collective-permute-start | bytes 1179656 | tf_op jit(solution)/shard_map/ppermute | solution.py:77
  147.0 3.5 %collective-permute-start.6 = (bf16[3,1,2,2,32,512]{5,4,3,2,0,1:T(8,128)(2,1)S(1)}, bf16[3,1,2,2,32,512]{5,4,3,2,0,1:T(8,128)(2,1)S(1)}, u32[]{:S(2)}, u32[]{:S(2)}) collective-permute-start(bf16[3,1,2,2,32,512]{5,4,3,2,0,1:T(8,128)(2,1)S(1)} %get-tuple-element.11), channel_id=1, source_target_pairs={{0,256},{128,384},{256,0},{384,128},{1,257},{129,385},{257,1},{385... | collective-permute-start | bytes 1179656 | tf_op jit(solution)/shard_map/ppermute | solution.py:77
  150.6 1.9 collective-permute-start.5
  152.5 3.6 %collective-permute-done.7 = bf16[3,1,2,2,32,512]{5,4,3,2,0,1:T(8,128)(2,1)S(1)} collective-permute-done((bf16[3,1,2,2,32,512]{5,4,3,2,0,1:T(8,128)(2,1)S(1)}, bf16[3,1,2,2,32,512]{5,4,3,2,0,1:T(8,128)(2,1)S(1)}, u32[]{:S(2)}, u32[]{:S(2)}) %collective-permute-start.7) | collective-permute-done | bytes 393248 | tf_op jit(solution)/shard_map/ppermute | solution.py:77
  156.1 4.5 %collective-permute-done.6 = bf16[3,1,2,2,32,512]{5,4,3,2,0,1:T(8,128)(2,1)S(1)} collective-permute-done((bf16[3,1,2,2,32,512]{5,4,3,2,0,1:T(8,128)(2,1)S(1)}, bf16[3,1,2,2,32,512]{5,4,3,2,0,1:T(8,128)(2,1)S(1)}, u32[]{:S(2)}, u32[]{:S(2)}) %collective-permute-start.6) | collective-permute-done | bytes 393248 | tf_op jit(solution)/shard_map/ppermute | solution.py:77
  160.6 9.4 %collective-permute-done.5 = bf16[3,1,2,2,32,512]{5,4,3,2,0,1:T(8,128)(2,1)S(1)} collective-permute-done((bf16[3,1,2,2,32,512]{5,4,3,2,0,1:T(8,128)(2,1)S(1)}, bf16[3,1,2,2,32,512]{5,4,3,2,0,1:T(8,128)(2,1)S(1)}, u32[]{:S(2)}, u32[]{:S(2)}) %collective-permute-start.5) | collective-permute-done | bytes 393248 | tf_op jit(solution)/shard_map/ppermute | solution.py:77
  170.2 1.8 gather_fusion.1
  172.0 1.6 bitcast_select_fusion
  173.7 2.2 %collective-permute-start.8 = (bf16[4,3,1,2,32,512]{5,4,3,1,0,2:T(8,128)(2,1)S(1)}, bf16[4,3,1,2,32,512]{5,4,3,1,0,2:T(8,128)(2,1)S(1)}, u32[]{:S(2)}, u32[]{:S(2)}) collective-permute-start(bf16[4,3,1,2,32,512]{5,4,3,1,0,2:T(8,128)(2,1)S(1)} %dynamic-slice_bitcast_fusion), channel_id=1, source_target_pairs={{0,64},{64,0},{1,65},{65,1},{2,66},{66,2},{3,67},{67,3},{4,68},{68... | collective-permute-start | bytes 2359304 | tf_op jit(solution)/shard_map/ppermute | solution.py:28
  175.9 19.1 %collective-permute-done.8 = bf16[4,3,1,2,32,512]{5,4,3,1,0,2:T(8,128)(2,1)S(1)} collective-permute-done((bf16[4,3,1,2,32,512]{5,4,3,1,0,2:T(8,128)(2,1)S(1)}, bf16[4,3,1,2,32,512]{5,4,3,1,0,2:T(8,128)(2,1)S(1)}, u32[]{:S(2)}, u32[]{:S(2)}) %collective-permute-start.8) | collective-permute-done | bytes 786464 | tf_op jit(solution)/shard_map/ppermute | solution.py:28
  195.2 2.8 %collective-permute-start.9 = (bf16[2,4,3,1,32,512]{5,4,2,1,0,3:T(8,128)(2,1)S(1)}, bf16[2,4,3,1,32,512]{5,4,2,1,0,3:T(8,128)(2,1)S(1)}, u32[]{:S(2)}, u32[]{:S(2)}) collective-permute-start(bf16[2,4,3,1,32,512]{5,4,2,1,0,3:T(8,128)(2,1)S(1)} %fusion.9), channel_id=1, source_target_pairs={{0,32},{32,0},{1,33},{33,1},{2,34},{34,2},{3,35},{35,3},{4,36},{36... | collective-permute-start | bytes 2359304 | tf_op jit(solution)/shard_map/ppermute | solution.py:28
  198.0 1.9 collective-permute-done.9
  200.3 2.0 copy.43
  202.2 3.3 %fusion = bf16[3,32,16,512]{3,1,2,0:T(8,128)(2,1)S(1)} fusion(f32[3,32,16,512]{3,1,2,0:T(8,128)} %bitcast.170, bf16[32,3,1,16,512]{4,3,1,2,0:T(8,128)(2,1)} %all-to-all-done.1), kind=kLoop, calls=%fused_computation.3 | loop fusion | flops 2359296 | bytes 6291456 | tf_op jit(solution)/shard_map/convert_element_type | solution.py:100
  205.5 2.0 copy.48
  (40 shorter events, 13.0 us)
Async XLA Ops:
  0.0 98.8 %copy-start = (bf16[512,512]{1,0:T(8,128)(2,1)S(1)}, bf16[512,512]{1,0:T(8,128)(2,1)}, u32[]{:S(2)}) copy-start(bf16[512,512]{1,0:T(8,128)(2,1)} %param.9) | copy-start | bytes 1572868
  2.7 93.3 %all-to-all-start = ((bf16[32,3,1,16,512]{4,3,1,2,0:T(8,128)(2,1)}), bf16[32,3,1,16,512]{4,3,1,2,0:T(8,128)(2,1)}, u32[]{:S(2)}, u32[]{:S(2)}) async-start(bf16[32,3,1,16,512]{4,3,1,2,0:T(8,128)(2,1)} %bitcast.165), calls=%async_computation | async-start | bytes 3145728 | tf_op jit(solution)/shard_map/all_to_all | solution.py:20
  23.6 5.0 %copy-start.1 = (bf16[3,32,16,512]{3,1,2,0:T(8,128)(2,1)}, bf16[3,32,16,512]{3,1,2,0:T(8,128)(2,1)S(1)}, u32[]{:S(2)}) copy-start(bf16[3,32,16,512]{3,1,2,0:T(8,128)(2,1)S(1)} %copy.32) | copy-start | bytes 4718596
  23.7 4.9 %collective-permute-start = (bf16[3,32,4,2,1,512]{5,1,3,2,0,4:T(8,128)(2,1)S(1)}, bf16[3,32,4,2,1,512]{5,1,3,2,0,4:T(8,128)(2,1)}, u32[]{:S(2)}, u32[]{:S(2)}) collective-permute-start(bf16[3,32,4,2,1,512]{5,1,3,2,0,4:T(8,128)(2,1)S(1)} %dynamic-slice_bitcast_fusion.1), channel_id=1, source_target_pairs={{0,32},{32,0},{1,33},{33,1},{2,34},{34,2},{3,35},{35,3},{4,36},{36... | collective-permute-start | bytes 2359304 | tf_op jit(solution)/shard_map/ppermute | solution.py:28
  32.3 77.9 %collective-permute-start.1 = (bf16[2,3,32,4,1,512]{5,2,3,1,0,4:T(8,128)(2,1)}, bf16[2,3,32,4,1,512]{5,2,3,1,0,4:T(8,128)(2,1)S(1)}, u32[]{:S(2)}, u32[]{:S(2)}) collective-permute-start(bf16[2,3,32,4,1,512]{5,2,3,1,0,4:T(8,128)(2,1)} %fusion.13), channel_id=1, source_target_pairs={{0,64},{64,0},{1,65},{65,1},{2,66},{66,2},{3,67},{67,3},{4,68},{68... | collective-permute-start | bytes 2359304 | tf_op jit(solution)/shard_map/ppermute | solution.py:28
  98.8 1.0 copy-start.3
  102.2 100.0 %all-to-all-start.1 = ((bf16[32,3,1,16,512]{4,3,1,2,0:T(8,128)(2,1)}), bf16[32,3,1,16,512]{4,3,1,2,0:T(8,128)(2,1)}, u32[]{:S(2)}, u32[]{:S(2)}) async-start(bf16[32,3,1,16,512]{4,3,1,2,0:T(8,128)(2,1)} %bitcast.174), calls=%async_computation.1 | async-start | bytes 3145728 | tf_op jit(solution)/shard_map/all_to_all | solution.py:20
  110.5 12.7 %collective-permute-start.2 = (bf16[2,2,3,32,1,512]{5,3,2,1,0,4:T(8,128)(2,1)S(1)}, bf16[2,2,3,32,1,512]{5,3,2,1,0,4:T(8,128)(2,1)S(1)}, u32[]{:S(2)}, u32[]{:S(2)}) collective-permute-start(bf16[2,2,3,32,1,512]{5,3,2,1,0,4:T(8,128)(2,1)S(1)} %get-tuple-element.14), channel_id=1, source_target_pairs={{0,128},{128,256},{256,384},{384,0},{1,129},{129,257},{257,385},{3... | collective-permute-start | bytes 1179656 | tf_op jit(solution)/shard_map/ppermute | solution.py:63
  113.7 19.1 %collective-permute-start.3 = (bf16[2,2,3,32,1,512]{5,3,2,1,0,4:T(8,128)(2,1)S(1)}, bf16[2,2,3,32,1,512]{5,3,2,1,0,4:T(8,128)(2,1)S(1)}, u32[]{:S(2)}, u32[]{:S(2)}) collective-permute-start(bf16[2,2,3,32,1,512]{5,3,2,1,0,4:T(8,128)(2,1)S(1)} %get-tuple-element.15), channel_id=1, source_target_pairs={{0,256},{128,384},{256,0},{384,128},{1,257},{129,385},{257,1},{385... | collective-permute-start | bytes 1179656 | tf_op jit(solution)/shard_map/ppermute | solution.py:63
  118.3 16.4 %collective-permute-start.4 = (bf16[2,2,3,32,1,512]{5,3,2,1,0,4:T(8,128)(2,1)S(1)}, bf16[2,2,3,32,1,512]{5,3,2,1,0,4:T(8,128)(2,1)S(1)}, u32[]{:S(2)}, u32[]{:S(2)}) collective-permute-start(bf16[2,2,3,32,1,512]{5,3,2,1,0,4:T(8,128)(2,1)S(1)} %get-tuple-element.16), channel_id=1, source_target_pairs={{0,384},{128,0},{256,128},{384,256},{1,385},{129,1},{257,129},{385... | collective-permute-start | bytes 1179656 | tf_op jit(solution)/shard_map/ppermute | solution.py:63
  138.4 1.0 copy-start.2
  139.4 1.0 copy-start.4
  141.6 14.5 %collective-permute-start.7 = (bf16[3,1,2,2,32,512]{5,4,3,2,0,1:T(8,128)(2,1)S(1)}, bf16[3,1,2,2,32,512]{5,4,3,2,0,1:T(8,128)(2,1)S(1)}, u32[]{:S(2)}, u32[]{:S(2)}) collective-permute-start(bf16[3,1,2,2,32,512]{5,4,3,2,0,1:T(8,128)(2,1)S(1)} %get-tuple-element.10), channel_id=1, source_target_pairs={{0,384},{128,0},{256,128},{384,256},{1,385},{129,1},{257,129},{385... | collective-permute-start | bytes 1179656 | tf_op jit(solution)/shard_map/ppermute | solution.py:77
  147.0 13.6 %collective-permute-start.6 = (bf16[3,1,2,2,32,512]{5,4,3,2,0,1:T(8,128)(2,1)S(1)}, bf16[3,1,2,2,32,512]{5,4,3,2,0,1:T(8,128)(2,1)S(1)}, u32[]{:S(2)}, u32[]{:S(2)}) collective-permute-start(bf16[3,1,2,2,32,512]{5,4,3,2,0,1:T(8,128)(2,1)S(1)} %get-tuple-element.11), channel_id=1, source_target_pairs={{0,256},{128,384},{256,0},{384,128},{1,257},{129,385},{257,1},{385... | collective-permute-start | bytes 1179656 | tf_op jit(solution)/shard_map/ppermute | solution.py:77
  150.6 19.4 %collective-permute-start.5 = (bf16[3,1,2,2,32,512]{5,4,3,2,0,1:T(8,128)(2,1)S(1)}, bf16[3,1,2,2,32,512]{5,4,3,2,0,1:T(8,128)(2,1)S(1)}, u32[]{:S(2)}, u32[]{:S(2)}) collective-permute-start(bf16[3,1,2,2,32,512]{5,4,3,2,0,1:T(8,128)(2,1)S(1)} %get-tuple-element.12), channel_id=1, source_target_pairs={{0,128},{128,256},{256,384},{384,0},{1,129},{129,257},{257,385},{3... | collective-permute-start | bytes 1179656 | tf_op jit(solution)/shard_map/ppermute | solution.py:77
  173.7 21.3 %collective-permute-start.8 = (bf16[4,3,1,2,32,512]{5,4,3,1,0,2:T(8,128)(2,1)S(1)}, bf16[4,3,1,2,32,512]{5,4,3,1,0,2:T(8,128)(2,1)S(1)}, u32[]{:S(2)}, u32[]{:S(2)}) collective-permute-start(bf16[4,3,1,2,32,512]{5,4,3,1,0,2:T(8,128)(2,1)S(1)} %dynamic-slice_bitcast_fusion), channel_id=1, source_target_pairs={{0,64},{64,0},{1,65},{65,1},{2,66},{66,2},{3,67},{67,3},{4,68},{68... | collective-permute-start | bytes 2359304 | tf_op jit(solution)/shard_map/ppermute | solution.py:28
  195.2 4.7 %collective-permute-start.9 = (bf16[2,4,3,1,32,512]{5,4,2,1,0,3:T(8,128)(2,1)S(1)}, bf16[2,4,3,1,32,512]{5,4,2,1,0,3:T(8,128)(2,1)S(1)}, u32[]{:S(2)}, u32[]{:S(2)}) collective-permute-start(bf16[2,4,3,1,32,512]{5,4,2,1,0,3:T(8,128)(2,1)S(1)} %fusion.9), channel_id=1, source_target_pairs={{0,32},{32,0},{1,33},{33,1},{2,34},{34,2},{3,35},{35,3},{4,36},{36... | collective-permute-start | bytes 2359304 | tf_op jit(solution)/shard_map/ppermute | solution.py:28
where the time goes:
time: 209 us; the launch traced here: 208 us
  waiting for transfers between devices  115 us (55%)
  starting transfers between devices  58.2 us (28%)
  local copies, waits for them, and re-layouts  17.9 us (9%)
  other arithmetic  11.8 us (6%)
  matrix products  3.93 us (2%)
    all_to_all x2, waiting for transfers between devices, exchange(): return lax.all_to_all(blocks, axes, split_axis=0, concat_axis=0, tiled=True)  61.6 us
    ppermute x6, waiting for transfers between devices, both_terms(): lax.ppermute(part, 'y', [(i, (i + s) % ny) for i in range(ny)])  30.8 us
    all_to_all x2, starting transfers between devices, exchange(): return lax.all_to_all(blocks, axes, split_axis=0, concat_axis=0, tiled=True)  26.5 us
    ppermute x4, waiting for transfers between devices, swap(): return lax.ppermute(x, axis, [(0, 1), (1, 0)])  23 us
    ppermute x6, starting transfers between devices, both_terms(): lax.ppermute(part, 'y', [(i, (i + s) % ny) for i in range(ny)])  21.6 us
    ppermute x4, starting transfers between devices, swap(): return lax.ppermute(x, axis, [(0, 1), (1, 0)])  10.1 us
    unnamed x12, local copies, waits for them, and re-layouts  5.99 us
  transfers between devices with their start and end apart: 12, of which 10 were waited for; matrix products, arithmetic and copies ran while one was open for 12% of the time, Pallas kernels for 0%

commit v1 on v0

--- a/solution.py
+++ b/solution.py
@@ -1,6 +1,7 @@
 import jax
 import jax.numpy as jnp
 from jax import lax
+from jax.experimental import pallas as pl
 from jax.sharding import Mesh, PartitionSpec as P
 
 
@@ -14,6 +15,21 @@
     curvature = jnp.einsum("ij,cjm->cim", diffusion, lines, preferred_element_type=jnp.float32)
     term = curvature - carrier[None].astype(jnp.float32) * gradient
     return term.astype(jnp.bfloat16)
+
+
+def copy_kernel(src_ref, out_ref):
+    out_ref[...] = src_ref[...]
+
+
+def in_output_layout(x):
+    block = pl.BlockSpec((1,) + x.shape[1:], lambda c: (c,) + (0,) * (x.ndim - 1))
+    return pl.pallas_call(
+        copy_kernel,
+        grid=(x.shape[0],),
+        in_specs=[block],
+        out_specs=block,
+        out_shape=jax.ShapeDtypeStruct(x.shape, x.dtype),
+    )(x)
 
 
 def exchange(blocks, axes):
@@ -83,6 +99,7 @@
     got = swap(take_at(b2, 1 - my_core, 4), "core")
     b1 = in_order(keep, got, my_core)
     wall_back = b1.transpose(3, 5, 2, 1, 0, 4, 6).reshape(comps, wall_local, span_local, stream_len)
+    wall_back = in_output_layout(wall_back)
 
     send = velocity.reshape(comps, column_count, ws, span_local, stream_len).transpose(1, 0, 2, 3, 4)
     got = exchange(send, COLS)

time: 209 us -> 210 us (level)
  waiting for transfers between devices: 115 us -> 111 us
  Pallas kernels: 0 us -> 3.37 us
    ppermute x6, waiting for transfers between devices: 30.8 us -> 26.7 us  [both_terms(): lax.ppermute(part, 'y', [(i, (i + s) % ny) for i in range(ny)])]
    convert_element_type x2 -> x0, local copies, waits for them, and re-layouts: 3.96 us -> none  [the longest x1 2.01 us: both_terms(): return summed.astype(jnp.bfloat16)]
    pallas_call x0 -> x1, Pallas kernels: none -> 3.37 us  [in_output_layout(): pl.pallas_call(copy_kernel, grid=(x.shape[0],), in_specs=[block], out_spe...]
  transfers between devices with their start and end apart: 12 -> 12, of which waited for: 10 -> 10; matrix products, arithmetic and copies ran while one was open for 12% -> 13% of each run, Pallas kernels for 0% -> 2%
where the time goes in v1:
time: 210 us; the launch traced here: 208 us
  waiting for transfers between devices  111 us (53%)
  starting transfers between devices  60.1 us (29%)
  local copies, waits for them, and re-layouts  17.5 us (8%)
  other arithmetic  12.1 us (6%)
  matrix products  3.93 us (2%)
  Pallas kernels  3.37 us (2%)
    all_to_all x2, waiting for transfers between devices, exchange(): return lax.all_to_all(blocks, axes, split_axis=0, concat_axis=0, tiled=True)  61.6 us
    ppermute x6, waiting for transfers between devices, both_terms(): lax.ppermute(part, 'y', [(i, (i + s) % ny) for i in range(ny)])  26.7 us
    all_to_all x2, starting transfers between devices, exchange(): return lax.all_to_all(blocks, axes, split_axis=0, concat_axis=0, tiled=True)  26.5 us
    ppermute x4, waiting for transfers between devices, swap(): return lax.ppermute(x, axis, [(0, 1), (1, 0)])  22.6 us
    ppermute x6, starting transfers between devices, both_terms(): lax.ppermute(part, 'y', [(i, (i + s) % ny) for i in range(ny)])  22.2 us
    ppermute x4, starting transfers between devices, swap(): return lax.ppermute(x, axis, [(0, 1), (1, 0)])  11.4 us
    unnamed x12, local copies, waits for them, and re-layouts  5.94 us
  transfers between devices with their start and end apart: 12, of which 10 were waited for; matrix products, arithmetic and copies ran while one was open for 13% of the time, Pallas kernels for 2%

profile of v1, /device:TPU:1, one launch (start us, length us, event | category | flops | bytes accessed | tf_op | source)
XLA Modules:
  0.0 208.3 jit_solution(11994014172740163597)
XLA Ops:
  0.0 2.7 %copy.53 = bf16[3,32,16,512]{3,2,0,1:T(8,128)(2,1)} copy(bf16[3,32,16,512]{3,2,1,0:T(8,128)(2,1)} %param.5) | data formatting | bytes 3145728 | tf_op args[0]
  2.7 18.6 %all-to-all-start = ((bf16[32,3,1,16,512]{4,3,1,2,0:T(8,128)(2,1)}), bf16[32,3,1,16,512]{4,3,1,2,0:T(8,128)(2,1)}, u32[]{:S(2)}, u32[]{:S(2)}) async-start(bf16[32,3,1,16,512]{4,3,1,2,0:T(8,128)(2,1)} %bitcast.166), calls=%async_computation | async-start | bytes 3145728 | tf_op jit(solution)/shard_map/all_to_all | solution.py:36
  21.3 2.3 %copy.33 = bf16[3,32,16,512]{3,1,2,0:T(8,128)(2,1)S(1)} copy(bf16[3,32,16,512]{3,2,1,0:T(8,128)(2,1)} %param.5) | data formatting | bytes 3145728 | tf_op args[0]
  23.7 2.9 %collective-permute-start = (bf16[3,32,4,2,1,512]{5,1,3,2,0,4:T(8,128)(2,1)S(1)}, bf16[3,32,4,2,1,512]{5,1,3,2,0,4:T(8,128)(2,1)}, u32[]{:S(2)}, u32[]{:S(2)}) collective-permute-start(bf16[3,32,4,2,1,512]{5,1,3,2,0,4:T(8,128)(2,1)S(1)} %dynamic-slice_bitcast_fusion.1), channel_id=1, source_target_pairs={{0,32},{32,0},{1,33},{33,1},{2,34},{34,2},{3,35},{35,3},{4,36},{36... | collective-permute-start | bytes 2359304 | tf_op jit(solution)/shard_map/ppermute | solution.py:44
  26.6 2.0 collective-permute-done
  32.3 2.2 %collective-permute-start.1 = (bf16[2,3,32,4,1,512]{5,2,3,1,0,4:T(8,128)(2,1)}, bf16[2,3,32,4,1,512]{5,2,3,1,0,4:T(8,128)(2,1)S(1)}, u32[]{:S(2)}, u32[]{:S(2)}) collective-permute-start(bf16[2,3,32,4,1,512]{5,2,3,1,0,4:T(8,128)(2,1)} %fusion.13), channel_id=1, source_target_pairs={{0,64},{64,0},{1,65},{65,1},{2,66},{66,2},{3,67},{67,3},{4,68},{68... | collective-permute-start | bytes 2359304 | tf_op jit(solution)/shard_map/ppermute | solution.py:44
  34.5 61.6 %all-to-all-done = bf16[32,3,1,16,512]{4,3,1,2,0:T(8,128)(2,1)} async-done(((bf16[32,3,1,16,512]{4,3,1,2,0:T(8,128)(2,1)}), bf16[32,3,1,16,512]{4,3,1,2,0:T(8,128)(2,1)}, u32[]{:S(2)}, u32[]{:S(2)}) %all-to-all-start) | async-done | bytes 1572896 | tf_op jit(solution)/shard_map/all_to_all | solution.py:36
  96.0 1.5 copy.46
  102.2 7.9 %all-to-all-start.1 = ((bf16[32,3,1,16,512]{4,3,1,2,0:T(8,128)(2,1)}), bf16[32,3,1,16,512]{4,3,1,2,0:T(8,128)(2,1)}, u32[]{:S(2)}, u32[]{:S(2)}) async-start(bf16[32,3,1,16,512]{4,3,1,2,0:T(8,128)(2,1)} %bitcast.174), calls=%async_computation.1 | async-start | bytes 3145728 | tf_op jit(solution)/shard_map/all_to_all | solution.py:36
  110.5 3.2 %collective-permute-start.2 = (bf16[2,2,3,32,1,512]{5,3,2,1,0,4:T(8,128)(2,1)S(1)}, bf16[2,2,3,32,1,512]{5,3,2,1,0,4:T(8,128)(2,1)S(1)}, u32[]{:S(2)}, u32[]{:S(2)}) collective-permute-start(bf16[2,2,3,32,1,512]{5,3,2,1,0,4:T(8,128)(2,1)S(1)} %get-tuple-element.14), channel_id=1, source_target_pairs={{0,128},{128,256},{256,384},{384,0},{1,129},{129,257},{257,385},{3... | collective-permute-start | bytes 1179656 | tf_op jit(solution)/shard_map/ppermute | solution.py:79
  113.7 4.5 %collective-permute-start.3 = (bf16[2,2,3,32,1,512]{5,3,2,1,0,4:T(8,128)(2,1)S(1)}, bf16[2,2,3,32,1,512]{5,3,2,1,0,4:T(8,128)(2,1)S(1)}, u32[]{:S(2)}, u32[]{:S(2)}) collective-permute-start(bf16[2,2,3,32,1,512]{5,3,2,1,0,4:T(8,128)(2,1)S(1)} %get-tuple-element.15), channel_id=1, source_target_pairs={{0,256},{128,384},{256,0},{384,128},{1,257},{129,385},{257,1},{385... | collective-permute-start | bytes 1179656 | tf_op jit(solution)/shard_map/ppermute | solution.py:79
  118.3 3.0 %collective-permute-start.4 = (bf16[2,2,3,32,1,512]{5,3,2,1,0,4:T(8,128)(2,1)S(1)}, bf16[2,2,3,32,1,512]{5,3,2,1,0,4:T(8,128)(2,1)S(1)}, u32[]{:S(2)}, u32[]{:S(2)}) collective-permute-start(bf16[2,2,3,32,1,512]{5,3,2,1,0,4:T(8,128)(2,1)S(1)} %get-tuple-element.16), channel_id=1, source_target_pairs={{0,384},{128,0},{256,128},{384,256},{1,385},{129,1},{257,129},{385... | collective-permute-start | bytes 1179656 | tf_op jit(solution)/shard_map/ppermute | solution.py:79
  121.3 2.0 collective-permute-done.2
  123.3 9.5 %collective-permute-done.3 = bf16[2,2,3,32,1,512]{5,3,2,1,0,4:T(8,128)(2,1)S(1)} collective-permute-done((bf16[2,2,3,32,1,512]{5,3,2,1,0,4:T(8,128)(2,1)S(1)}, bf16[2,2,3,32,1,512]{5,3,2,1,0,4:T(8,128)(2,1)S(1)}, u32[]{:S(2)}, u32[]{:S(2)}) %collective-permute-start.3) | collective-permute-done | bytes 393248 | tf_op jit(solution)/shard_map/ppermute | solution.py:79
  132.8 1.8 collective-permute-done.4
  134.8 1.8 gather_fusion
  136.6 1.6 fusion.5
  141.6 5.3 %collective-permute-start.5 = (bf16[3,1,2,2,32,512]{5,4,3,2,0,1:T(8,128)(2,1)S(1)}, bf16[3,1,2,2,32,512]{5,4,3,2,0,1:T(8,128)(2,1)S(1)}, u32[]{:S(2)}, u32[]{:S(2)}) collective-permute-start(bf16[3,1,2,2,32,512]{5,4,3,2,0,1:T(8,128)(2,1)S(1)} %get-tuple-element.12), channel_id=1, source_target_pairs={{0,128},{128,256},{256,384},{384,0},{1,129},{129,257},{257,385},{3... | collective-permute-start | bytes 1179656 | tf_op jit(solution)/shard_map/ppermute | solution.py:93
  146.9 3.2 %collective-permute-start.6 = (bf16[3,1,2,2,32,512]{5,4,3,2,0,1:T(8,128)(2,1)S(1)}, bf16[3,1,2,2,32,512]{5,4,3,2,0,1:T(8,128)(2,1)S(1)}, u32[]{:S(2)}, u32[]{:S(2)}) collective-permute-start(bf16[3,1,2,2,32,512]{5,4,3,2,0,1:T(8,128)(2,1)S(1)} %get-tuple-element.11), channel_id=1, source_target_pairs={{0,256},{128,384},{256,0},{384,128},{1,257},{129,385},{257,1},{385... | collective-permute-start | bytes 1179656 | tf_op jit(solution)/shard_map/ppermute | solution.py:93
  150.1 3.0 %collective-permute-start.7 = (bf16[3,1,2,2,32,512]{5,4,3,2,0,1:T(8,128)(2,1)S(1)}, bf16[3,1,2,2,32,512]{5,4,3,2,0,1:T(8,128)(2,1)S(1)}, u32[]{:S(2)}, u32[]{:S(2)}) collective-permute-start(bf16[3,1,2,2,32,512]{5,4,3,2,0,1:T(8,128)(2,1)S(1)} %get-tuple-element.10), channel_id=1, source_target_pairs={{0,384},{128,0},{256,128},{384,256},{1,385},{129,1},{257,129},{385... | collective-permute-start | bytes 1179656 | tf_op jit(solution)/shard_map/ppermute | solution.py:93
  153.1 2.5 %collective-permute-done.5 = bf16[3,1,2,2,32,512]{5,4,3,2,0,1:T(8,128)(2,1)S(1)} collective-permute-done((bf16[3,1,2,2,32,512]{5,4,3,2,0,1:T(8,128)(2,1)S(1)}, bf16[3,1,2,2,32,512]{5,4,3,2,0,1:T(8,128)(2,1)S(1)}, u32[]{:S(2)}, u32[]{:S(2)}) %collective-permute-start.5) | collective-permute-done | bytes 393248 | tf_op jit(solution)/shard_map/ppermute | solution.py:93
  155.6 9.9 %collective-permute-done.6 = bf16[3,1,2,2,32,512]{5,4,3,2,0,1:T(8,128)(2,1)S(1)} collective-permute-done((bf16[3,1,2,2,32,512]{5,4,3,2,0,1:T(8,128)(2,1)S(1)}, bf16[3,1,2,2,32,512]{5,4,3,2,0,1:T(8,128)(2,1)S(1)}, u32[]{:S(2)}, u32[]{:S(2)}) %collective-permute-start.6) | collective-permute-done | bytes 393248 | tf_op jit(solution)/shard_map/ppermute | solution.py:93
  166.7 1.8 gather_fusion.1
  168.5 1.6 bitcast_select_fusion
  170.2 2.2 %collective-permute-start.8 = (bf16[4,3,1,2,32,512]{5,4,3,1,0,2:T(8,128)(2,1)S(1)}, bf16[4,3,1,2,32,512]{5,4,3,1,0,2:T(8,128)(2,1)S(1)}, u32[]{:S(2)}, u32[]{:S(2)}) collective-permute-start(bf16[4,3,1,2,32,512]{5,4,3,1,0,2:T(8,128)(2,1)S(1)} %dynamic-slice_bitcast_fusion), channel_id=1, source_target_pairs={{0,64},{64,0},{1,65},{65,1},{2,66},{66,2},{3,67},{67,3},{4,68},{68... | collective-permute-start | bytes 2359304 | tf_op jit(solution)/shard_map/ppermute | solution.py:44
  172.4 18.7 %collective-permute-done.8 = bf16[4,3,1,2,32,512]{5,4,3,1,0,2:T(8,128)(2,1)S(1)} collective-permute-done((bf16[4,3,1,2,32,512]{5,4,3,1,0,2:T(8,128)(2,1)S(1)}, bf16[4,3,1,2,32,512]{5,4,3,1,0,2:T(8,128)(2,1)S(1)}, u32[]{:S(2)}, u32[]{:S(2)}) %collective-permute-start.8) | collective-permute-done | bytes 786464 | tf_op jit(solution)/shard_map/ppermute | solution.py:44
  191.3 4.1 %collective-permute-start.9 = (bf16[2,4,3,1,32,512]{5,4,2,1,0,3:T(8,128)(2,1)S(1)}, bf16[2,4,3,1,32,512]{5,4,2,1,0,3:T(8,128)(2,1)S(1)}, u32[]{:S(2)}, u32[]{:S(2)}) collective-permute-start(bf16[2,4,3,1,32,512]{5,4,2,1,0,3:T(8,128)(2,1)S(1)} %fusion.9), channel_id=1, source_target_pairs={{0,32},{32,0},{1,33},{33,1},{2,34},{34,2},{3,35},{35,3},{4,36},{36... | collective-permute-start | bytes 2359304 | tf_op jit(solution)/shard_map/ppermute | solution.py:44
  195.4 1.9 collective-permute-done.9
  197.6 1.6 copy.44
  199.2 2.0 reshape.105.src_ref
  201.2 3.4 %shard_map.55 = bf16[3,32,16,512]{3,2,1,0:T(8,128)(2,1)} custom-call(bf16[3,32,16,512]{3,2,1,0:T(8,128)(2,1)} %reshape.105.src_ref), custom_call_target="tpu_custom_call" | custom-call | tf_op jit(solution)/shard_map/pallas_call | solution.py:26
  204.6 3.7 %fusion = bf16[3,32,16,512]{3,2,1,0:T(8,128)(2,1)} fusion(bf16[3,32,16,512]{3,2,1,0:T(8,128)(2,1)} %shard_map.55, bf16[32,3,1,16,512]{4,3,1,2,0:T(8,128)(2,1)} %all-to-all-done.1), kind=kLoop, calls=%fused_computation.3 | loop fusion | flops 3145728 | bytes 4718592 | tf_op jit(solution)/shard_map/convert_element_type | solution.py:117
  (41 shorter events, 13.8 us)
Async XLA Ops:
  0.0 98.8 %copy-start = (bf16[512,512]{1,0:T(8,128)(2,1)S(1)}, bf16[512,512]{1,0:T(8,128)(2,1)}, u32[]{:S(2)}) copy-start(bf16[512,512]{1,0:T(8,128)(2,1)} %param.9) | copy-start | bytes 1572868
  2.7 93.3 %all-to-all-start = ((bf16[32,3,1,16,512]{4,3,1,2,0:T(8,128)(2,1)}), bf16[32,3,1,16,512]{4,3,1,2,0:T(8,128)(2,1)}, u32[]{:S(2)}, u32[]{:S(2)}) async-start(bf16[32,3,1,16,512]{4,3,1,2,0:T(8,128)(2,1)} %bitcast.166), calls=%async_computation | async-start | bytes 3145728 | tf_op jit(solution)/shard_map/all_to_all | solution.py:36
  23.6 5.0 %copy-start.1 = (bf16[3,32,16,512]{3,1,2,0:T(8,128)(2,1)}, bf16[3,32,16,512]{3,1,2,0:T(8,128)(2,1)S(1)}, u32[]{:S(2)}) copy-start(bf16[3,32,16,512]{3,1,2,0:T(8,128)(2,1)S(1)} %copy.33) | copy-start | bytes 4718596
  23.7 4.9 %collective-permute-start = (bf16[3,32,4,2,1,512]{5,1,3,2,0,4:T(8,128)(2,1)S(1)}, bf16[3,32,4,2,1,512]{5,1,3,2,0,4:T(8,128)(2,1)}, u32[]{:S(2)}, u32[]{:S(2)}) collective-permute-start(bf16[3,32,4,2,1,512]{5,1,3,2,0,4:T(8,128)(2,1)S(1)} %dynamic-slice_bitcast_fusion.1), channel_id=1, source_target_pairs={{0,32},{32,0},{1,33},{33,1},{2,34},{34,2},{3,35},{35,3},{4,36},{36... | collective-permute-start | bytes 2359304 | tf_op jit(solution)/shard_map/ppermute | solution.py:44
  32.3 77.9 %collective-permute-start.1 = (bf16[2,3,32,4,1,512]{5,2,3,1,0,4:T(8,128)(2,1)}, bf16[2,3,32,4,1,512]{5,2,3,1,0,4:T(8,128)(2,1)S(1)}, u32[]{:S(2)}, u32[]{:S(2)}) collective-permute-start(bf16[2,3,32,4,1,512]{5,2,3,1,0,4:T(8,128)(2,1)} %fusion.13), channel_id=1, source_target_pairs={{0,64},{64,0},{1,65},{65,1},{2,66},{66,2},{3,67},{67,3},{4,68},{68... | collective-permute-start | bytes 2359304 | tf_op jit(solution)/shard_map/ppermute | solution.py:44
  98.8 1.0 copy-start.3
  102.2 102.4 %all-to-all-start.1 = ((bf16[32,3,1,16,512]{4,3,1,2,0:T(8,128)(2,1)}), bf16[32,3,1,16,512]{4,3,1,2,0:T(8,128)(2,1)}, u32[]{:S(2)}, u32[]{:S(2)}) async-start(bf16[32,3,1,16,512]{4,3,1,2,0:T(8,128)(2,1)} %bitcast.174), calls=%async_computation.1 | async-start | bytes 3145728 | tf_op jit(solution)/shard_map/all_to_all | solution.py:36
  110.5 12.7 %collective-permute-start.2 = (bf16[2,2,3,32,1,512]{5,3,2,1,0,4:T(8,128)(2,1)S(1)}, bf16[2,2,3,32,1,512]{5,3,2,1,0,4:T(8,128)(2,1)S(1)}, u32[]{:S(2)}, u32[]{:S(2)}) collective-permute-start(bf16[2,2,3,32,1,512]{5,3,2,1,0,4:T(8,128)(2,1)S(1)} %get-tuple-element.14), channel_id=1, source_target_pairs={{0,128},{128,256},{256,384},{384,0},{1,129},{129,257},{257,385},{3... | collective-permute-start | bytes 1179656 | tf_op jit(solution)/shard_map/ppermute | solution.py:79
  113.7 19.1 %collective-permute-start.3 = (bf16[2,2,3,32,1,512]{5,3,2,1,0,4:T(8,128)(2,1)S(1)}, bf16[2,2,3,32,1,512]{5,3,2,1,0,4:T(8,128)(2,1)S(1)}, u32[]{:S(2)}, u32[]{:S(2)}) collective-permute-start(bf16[2,2,3,32,1,512]{5,3,2,1,0,4:T(8,128)(2,1)S(1)} %get-tuple-element.15), channel_id=1, source_target_pairs={{0,256},{128,384},{256,0},{384,128},{1,257},{129,385},{257,1},{385... | collective-permute-start | bytes 1179656 | tf_op jit(solution)/shard_map/ppermute | solution.py:79
  118.3 16.4 %collective-permute-start.4 = (bf16[2,2,3,32,1,512]{5,3,2,1,0,4:T(8,128)(2,1)S(1)}, bf16[2,2,3,32,1,512]{5,3,2,1,0,4:T(8,128)(2,1)S(1)}, u32[]{:S(2)}, u32[]{:S(2)}) collective-permute-start(bf16[2,2,3,32,1,512]{5,3,2,1,0,4:T(8,128)(2,1)S(1)} %get-tuple-element.16), channel_id=1, source_target_pairs={{0,384},{128,0},{256,128},{384,256},{1,385},{129,1},{257,129},{385... | collective-permute-start | bytes 1179656 | tf_op jit(solution)/shard_map/ppermute | solution.py:79
  138.4 1.0 copy-start.2
  139.4 1.0 copy-start.4
  141.6 14.0 %collective-permute-start.5 = (bf16[3,1,2,2,32,512]{5,4,3,2,0,1:T(8,128)(2,1)S(1)}, bf16[3,1,2,2,32,512]{5,4,3,2,0,1:T(8,128)(2,1)S(1)}, u32[]{:S(2)}, u32[]{:S(2)}) collective-permute-start(bf16[3,1,2,2,32,512]{5,4,3,2,0,1:T(8,128)(2,1)S(1)} %get-tuple-element.12), channel_id=1, source_target_pairs={{0,128},{128,256},{256,384},{384,0},{1,129},{129,257},{257,385},{3... | collective-permute-start | bytes 1179656 | tf_op jit(solution)/shard_map/ppermute | solution.py:93
  146.9 18.7 %collective-permute-start.6 = (bf16[3,1,2,2,32,512]{5,4,3,2,0,1:T(8,128)(2,1)S(1)}, bf16[3,1,2,2,32,512]{5,4,3,2,0,1:T(8,128)(2,1)S(1)}, u32[]{:S(2)}, u32[]{:S(2)}) collective-permute-start(bf16[3,1,2,2,32,512]{5,4,3,2,0,1:T(8,128)(2,1)S(1)} %get-tuple-element.11), channel_id=1, source_target_pairs={{0,256},{128,384},{256,0},{384,128},{1,257},{129,385},{257,1},{385... | collective-permute-start | bytes 1179656 | tf_op jit(solution)/shard_map/ppermute | solution.py:93
  150.1 16.4 %collective-permute-start.7 = (bf16[3,1,2,2,32,512]{5,4,3,2,0,1:T(8,128)(2,1)S(1)}, bf16[3,1,2,2,32,512]{5,4,3,2,0,1:T(8,128)(2,1)S(1)}, u32[]{:S(2)}, u32[]{:S(2)}) collective-permute-start(bf16[3,1,2,2,32,512]{5,4,3,2,0,1:T(8,128)(2,1)S(1)} %get-tuple-element.10), channel_id=1, source_target_pairs={{0,384},{128,0},{256,128},{384,256},{1,385},{129,1},{257,129},{385... | collective-permute-start | bytes 1179656 | tf_op jit(solution)/shard_map/ppermute | solution.py:93
  170.2 20.9 %collective-permute-start.8 = (bf16[4,3,1,2,32,512]{5,4,3,1,0,2:T(8,128)(2,1)S(1)}, bf16[4,3,1,2,32,512]{5,4,3,1,0,2:T(8,128)(2,1)S(1)}, u32[]{:S(2)}, u32[]{:S(2)}) collective-permute-start(bf16[4,3,1,2,32,512]{5,4,3,1,0,2:T(8,128)(2,1)S(1)} %dynamic-slice_bitcast_fusion), channel_id=1, source_target_pairs={{0,64},{64,0},{1,65},{65,1},{2,66},{66,2},{3,67},{67,3},{4,68},{68... | collective-permute-start | bytes 2359304 | tf_op jit(solution)/shard_map/ppermute | solution.py:44
  191.3 6.0 %collective-permute-start.9 = (bf16[2,4,3,1,32,512]{5,4,2,1,0,3:T(8,128)(2,1)S(1)}, bf16[2,4,3,1,32,512]{5,4,2,1,0,3:T(8,128)(2,1)S(1)}, u32[]{:S(2)}, u32[]{:S(2)}) collective-permute-start(bf16[2,4,3,1,32,512]{5,4,2,1,0,3:T(8,128)(2,1)S(1)} %fusion.9), channel_id=1, source_target_pairs={{0,32},{32,0},{1,33},{33,1},{2,34},{34,2},{3,35},{35,3},{4,36},{36... | collective-permute-start | bytes 2359304 | tf_op jit(solution)/shard_map/ppermute | solution.py:44
